TPU v7x, 128 devices: a whole 4x4x4 slice. The times are simulated.
128 devices in a mesh: dp: 2 (over core), cent: 64 (over z, y, x).
Axes of the slice: x: 4, y: 4, z: 4, core: 2. Of those that a mesh axis runs over, the one named last changes fastest.
Arguments:
- points: bfloat16 [16384, 768], P(('dp', 'cent')), may hold values from -16 to 16
- centroids: float32 [32768, 768], P(('dp', 'cent')), may hold values from -1.5 to 1.5
Outputs:
- new_centroids: float32 [32768, 768], P(('dp', 'cent'))
- log_total: float32 [16384], P(('dp', 'cent'))
All inputs are finite; a program needn't handle non-finite values.
Results may differ from a plain program's by a relative error of at most 0.0088.
Values may be sent and summed in bfloat16 or wider, within the bound.
No kernel may reach another device: no remote copies, remote signals or barrier semaphores. Data moves between devices by JAX's collectives and lax.ppermute only.
A program may use at most 128 MiB of HBM per device.

v0:
```python
import math
import jax
import jax.numpy as jnp
from jax import lax
from jax.sharding import PartitionSpec as P

HALVES = 2


def score_block(members, cent_block, score_scale):
    sq_norm = jnp.sum(jnp.square(cent_block.astype(jnp.float32)), axis=1)
    products = lax.dot_general(
        members, cent_block, (((1,), (1,)), ((), ())), preferred_element_type=jnp.float32
    )
    return (2.0 * products - sq_norm[None, :]) * score_scale


def group_log_total(local_max, local_sum, own_points):
    cent_count = lax.axis_size("cent")
    packed = jnp.stack(
        [local_max.reshape(cent_count, own_points), local_sum.reshape(cent_count, own_points)],
        axis=1,
    )
    parts = lax.all_to_all(packed, "cent", 0, 0, tiled=True)
    part_max, part_sum = (parts[:, 0], parts[:, 1])
    top = jnp.max(part_max, axis=0)
    total = jnp.sum(part_sum * jnp.exp(part_max - top[None, :]), axis=0)
    own_total = top + jnp.log(total)
    spread = jnp.broadcast_to(own_total[None], (cent_count, own_points))
    log_total = lax.all_to_all(spread, "cent", 0, 0, tiled=True).reshape(cent_count * own_points)
    return (own_total, log_total)


def on_device(points, centroids):
    feature_width = centroids.shape[1]
    own_points = points.shape[0]
    cent_count = lax.axis_size("cent")
    score_scale = 7.0 / math.sqrt(feature_width)
    copies = centroids.astype(jnp.bfloat16)
    members = lax.all_gather(points, "cent", axis=0, tiled=True)
    gathered = lax.all_gather(copies, "dp", axis=0, tiled=True)
    half_points = own_points // HALVES
    split = members.reshape(cent_count, HALVES, half_points, feature_width)
    own_parts = []
    sums = None
    counts = None
    for index_h in range(HALVES):
        half = split[:, index_h].reshape(cent_count * half_points, feature_width)
        scores = score_block(half, gathered, score_scale)
        local_max = jnp.max(scores, axis=1)
        local_sum = jnp.sum(jnp.exp(scores - local_max[:, None]), axis=1)
        own_total, log_total = group_log_total(local_max, local_sum, half_points)
        own_parts.append(own_total)
        weights = jnp.exp(scores - log_total[:, None]).astype(jnp.bfloat16)
        part_sums = lax.dot_general(
            weights, half, (((0,), (0,)), ((), ())), preferred_element_type=jnp.float32
        )
        part_counts = jnp.sum(weights, axis=0, dtype=jnp.float32)
        sums = part_sums if sums is None else sums + part_sums
        counts = part_counts if counts is None else counts + part_counts
    own_sums = lax.psum_scatter(sums, "dp", scatter_dimension=0, tiled=True)
    own_counts = lax.psum_scatter(counts, "dp", scatter_dimension=0, tiled=True)
    new_centroids = (own_sums + centroids) / (own_counts[:, None] + 1.0)
    return (new_centroids, jnp.concatenate(own_parts))


def solution(mesh):
    placed = (P(("dp", "cent"), None), P(("dp", "cent"), None))
    return jax.shard_map(
        on_device,
        mesh=mesh,
        in_specs=placed,
        out_specs=(P(("dp", "cent"), None), P(("dp", "cent"))),
        check_vma=False,
    )
```

profile of v0, /device:TPU:1, one launch (start us, length us, event | category | flops | bytes accessed | tf_op | source)
XLA Modules:
  0.0 230.5 jit_solution(3304867153175038017)
XLA Ops:
  7.2 0.7 all-gather.2.cloned.1.call-update
  7.9 1.2 convert_element_type.19
  9.1 3.4 %all_gather.7 = bf16[512,768]{1,0:T(8,128)(2,1)S(1)} all-gather(bf16[256,768]{1,0:T(8,128)(2,1)S(1)} %convert_element_type.19), channel_id=1, replica_groups=mesh['dp'=2,'cent'=64] {'dp'}, dimensions={0}, use_global_device_ids=true | all-gather | bytes 1179648 | tf_op jit(solution)/shard_map/all_gather | solution.py:41
  12.7 92.0 %all-gather.2.cloned.1.call-done = bf16[8192,768]{1,0:T(8,128)(2,1)} async-done(((bf16[128,768]{1,0:T(8,128)(2,1)}), bf16[8192,768]{1,0:T(8,128)(2,1)}) %all-gather.2.cloned.1.call-update) | async-done | bytes 12582928 | tf_op jit(solution)/shard_map/all_gather | solution.py:40
  104.7 8.6 %fusion.1 = (bf16[64,1,64,768]{3,2,1,0:T(8,128)(2,1)}, bf16[64,1,64,768]{3,2,1,0:T(8,128)(2,1)S(1)}) fusion(bf16[64,2,64,768]{3,2,1,0:T(8,128)(2,1)} %bitcast.18), kind=kLoop, calls=%fused_computation.20 | loop fusion | bytes 25165824 | tf_op jit(solution)/shard_map/slice | solution.py:48
  113.4 5.8 %fusion.4 = (f32[4096]{0:T(1024)S(1)}, f32[4096,512]{0,1:T(8,128)}) fusion(f32[512]{0:T(512)S(1)} %multiply_reduce_fusion, bf16[4096,768]{1,0:T(8,128)(2,1)S(1)} %bitcast.21, bf16[512,768]{1,0:T(8,128)(2,1)S(1)} %all_gather.7), kind=kOutput, calls=%fused_computation.23 | convolution fusion | flops 3229609984 | bytes 15484928 | tf_op jit(solution)/shard_map/dot_general | solution.py:12
  119.2 4.5 %exponential_reduce_fusion.1 = f32[4096]{0:T(1024)S(1)} fusion(f32[4096,512]{0,1:T(8,128)} %get-tuple-element.9, f32[4096]{0:T(1024)S(1)} %get-tuple-element.8), kind=kLoop, calls=%fused_computation.6 | loop fusion | flops 4190208 | bytes 8421376 | tf_op jit(solution)/shard_map/reduce_sum | solution.py:51
  123.9 0.7 reshape.60
  124.7 8.3 %all-to-all-start = ((f32[64,1,128]{2,1,0:T(1,128)}), f32[64,1,128]{2,1,0:T(1,128)S(1)}, u32[]{:S(2)}, u32[]{:S(2)}) async-start(f32[64,1,128]{2,1,0:T(1,128)} %reshape.60), calls=%async_computation | async-start | bytes 65536 | tf_op jit(solution)/shard_map/all_to_all | solution.py:24
  133.0 8.5 %fusion.5 = (f32[4096]{0:T(1024)S(1)}, f32[4096,512]{0,1:T(8,128)}) fusion(f32[512]{0:T(512)S(1)} %multiply_reduce_fusion, bf16[4096,768]{1,0:T(8,128)(2,1)} %bitcast.19, bf16[512,768]{1,0:T(8,128)(2,1)S(1)} %all_gather.7), kind=kOutput, calls=%fused_computation.24 | convolution fusion | flops 3229609984 | bytes 15484928 | tf_op jit(solution)/shard_map/dot_general | solution.py:12
  141.6 4.5 %exponential_reduce_fusion = f32[4096]{0:T(1024)S(1)} fusion(f32[4096,512]{0,1:T(8,128)} %get-tuple-element.11, f32[4096]{0:T(1024)S(1)} %get-tuple-element.10), kind=kLoop, calls=%fused_computation.3 | loop fusion | flops 4190208 | bytes 8421376 | tf_op jit(solution)/shard_map/reduce_sum | solution.py:51
  146.3 0.7 reshape.62
  147.0 9.8 %all-to-all-start.2 = ((f32[64,1,128]{2,1,0:T(1,128)}), f32[64,1,128]{2,1,0:T(1,128)S(1)}, u32[]{:S(2)}, u32[]{:S(2)}) async-start(f32[64,1,128]{2,1,0:T(1,128)} %reshape.62), calls=%async_computation.2 | async-start | bytes 65536 | tf_op jit(solution)/shard_map/all_to_all | solution.py:24
  156.8 0.5 broadcast.35
  157.3 0.7 reduce.10
  158.3 7.0 %all-to-all-done.2 = f32[64,1,128]{2,1,0:T(1,128)S(1)} async-done(((f32[64,1,128]{2,1,0:T(1,128)}), f32[64,1,128]{2,1,0:T(1,128)S(1)}, u32[]{:S(2)}, u32[]{:S(2)}) %all-to-all-start.2) | async-done | bytes 32800 | tf_op jit(solution)/shard_map/all_to_all | solution.py:24
  165.2 0.6 broadcast_in_dim.4
  165.8 4.7 %all-to-all-start.1 = ((f32[64,1,64]{2,1,0:T(1,128)}), f32[64,1,64]{2,1,0:T(1,128)S(1)}, u32[]{:S(2)}, u32[]{:S(2)}) async-start(f32[64,1,64]{2,1,0:T(1,128)} %broadcast_in_dim.4), calls=%async_computation.1 | async-start | bytes 65536 | tf_op jit(solution)/shard_map/all_to_all | solution.py:30
  170.5 0.7 reduce.11
  171.5 7.4 %all-to-all-done.1 = f32[64,1,64]{2,1,0:T(1,128)S(1)} async-done(((f32[64,1,64]{2,1,0:T(1,128)}), f32[64,1,64]{2,1,0:T(1,128)S(1)}, u32[]{:S(2)}, u32[]{:S(2)}) %all-to-all-start.1) | async-done | bytes 16416 | tf_op jit(solution)/shard_map/all_to_all | solution.py:30
  178.9 0.6 broadcast_in_dim.5
  179.5 4.7 %all-to-all-start.3 = ((f32[64,1,64]{2,1,0:T(1,128)}), f32[64,1,64]{2,1,0:T(1,128)S(1)}, u32[]{:S(2)}, u32[]{:S(2)}) async-start(f32[64,1,64]{2,1,0:T(1,128)} %broadcast_in_dim.5), calls=%async_computation.3 | async-start | bytes 65536 | tf_op jit(solution)/shard_map/all_to_all | solution.py:30
  185.0 0.7 reduce.8
  185.8 7.7 %fusion = f32[512,768]{1,0:T(8,128)S(1)} fusion(bf16[4096,768]{1,0:T(8,128)(2,1)} %bitcast.22, f32[4096,512]{0,1:T(8,128)} %get-tuple-element.9, f32[4096]{0:T(1024)S(1)} %sub.72), kind=kOutput, calls=%fused_computation.10 | convolution fusion | flops 3225419776 | bytes 16269312 | tf_op jit(solution)/shard_map/dot_general | solution.py:55
  193.5 0.7 reduce.9
  194.3 9.8 %convolution_add_fusion = f32[512,768]{1,0:T(8,128)} fusion(f32[512,768]{1,0:T(8,128)S(1)} %fusion, bf16[4096,768]{1,0:T(8,128)(2,1)} %bitcast.20, f32[4096,512]{0,1:T(8,128)} %get-tuple-element.11, f32[4096]{0:T(1024)S(1)} %sub.80), kind=kOutput, calls=%fused_computation.9 | convolution fusion | flops 3225812992 | bytes 17842176 | tf_op jit(solution)/shard_map/dot_general | solution.py:55
  204.1 0.6 dynamic-slice
  205.4 0.6 pad_maximum_fusion.2
  205.9 7.1 %convert_reduce_fusion = (f32[512]{0:T(512)S(1)}, f32[512]{0:T(512)S(1)}) fusion(f32[4096,512]{0,1:T(8,128)} %get-tuple-element.11, f32[4096]{0:T(1024)S(1)} %sub.80, f32[4096,512]{0,1:T(8,128)} %get-tuple-element.9, f32[4096]{0:T(1024)S(1)} %sub.72), kind=kLoop, calls=%fused_computation | loop fusion | flops 16776192 | bytes 16814080 | tf_op jit(solution)/shard_map/reduce_sum | solution.py:58
  213.1 6.9 %all-reduce = f32[512]{0:T(512)S(1)} all-reduce(f32[512]{0:T(512)S(1)} %add.38), channel_id=3, replica_groups=mesh['dp'=2,'cent'=64] {'dp'}, use_global_device_ids=true, to_apply=%region_12.0.clone | all-reduce | flops 512 | bytes 4096
  220.0 1.4 reduce-scatter.2.cloned.1.call-done
  221.5 2.1 add_divide_fusion
  (33 shorter events, 2.2 us)
Async XLA Ops:
  7.2 97.6 %all-gather.2.cloned.1.call-start = ((), (), s32[]{:S(2)}) async-start(), calls=%async_computation.5 | async-start | bytes 12779520 | tf_op jit(solution)/shard_map/all_gather | solution.py:40
  113.4 5.8 %copy-start = (bf16[64,1,64,768]{3,2,1,0:T(8,128)(2,1)}, bf16[64,1,64,768]{3,2,1,0:T(8,128)(2,1)S(1)}, u32[]{:S(2)}) copy-start(bf16[64,1,64,768]{3,2,1,0:T(8,128)(2,1)S(1)} %get-tuple-element.3) | copy-start | bytes 18874372
  124.7 22.3 %all-to-all-start = ((f32[64,1,128]{2,1,0:T(1,128)}), f32[64,1,128]{2,1,0:T(1,128)S(1)}, u32[]{:S(2)}, u32[]{:S(2)}) async-start(f32[64,1,128]{2,1,0:T(1,128)} %reshape.60), calls=%async_computation | async-start | bytes 65536 | tf_op jit(solution)/shard_map/all_to_all | solution.py:24
  147.0 18.2 %all-to-all-start.2 = ((f32[64,1,128]{2,1,0:T(1,128)}), f32[64,1,128]{2,1,0:T(1,128)S(1)}, u32[]{:S(2)}, u32[]{:S(2)}) async-start(f32[64,1,128]{2,1,0:T(1,128)} %reshape.62), calls=%async_computation.2 | async-start | bytes 65536 | tf_op jit(solution)/shard_map/all_to_all | solution.py:24
  165.8 13.0 %all-to-all-start.1 = ((f32[64,1,64]{2,1,0:T(1,128)}), f32[64,1,64]{2,1,0:T(1,128)S(1)}, u32[]{:S(2)}, u32[]{:S(2)}) async-start(f32[64,1,64]{2,1,0:T(1,128)} %broadcast_in_dim.4), calls=%async_computation.1 | async-start | bytes 65536 | tf_op jit(solution)/shard_map/all_to_all | solution.py:30
  179.5 14.0 %all-to-all-start.3 = ((f32[64,1,64]{2,1,0:T(1,128)}), f32[64,1,64]{2,1,0:T(1,128)S(1)}, u32[]{:S(2)}, u32[]{:S(2)}) async-start(f32[64,1,64]{2,1,0:T(1,128)} %broadcast_in_dim.5), calls=%async_computation.3 | async-start | bytes 65536 | tf_op jit(solution)/shard_map/all_to_all | solution.py:30
  184.2 37.3 %reduce-scatter.2.cloned.1.call-start = ((), (), s32[]{:S(2)}) async-start(), calls=%async_computation.6 | async-start | bytes 2359296 | tf_op jit(solution)/shard_map/reduce_scatter | solution.py:61
  194.3 9.8 %copy-start.2 = (u32[128]{0:T(128)S(1)}, u32[128]{0:T(128)}, u32[]{:S(2)}) copy-start(u32[128]{0:T(128)} %constant.12) | copy-start | bytes 1540
  205.9 15.5 %copy-start.1 = (f32[256,768]{1,0:T(8,128)S(1)}, f32[256,768]{1,0:T(8,128)}, u32[]{:S(2)}) copy-start(f32[256,768]{1,0:T(8,128)} %param.3) | copy-start | bytes 2359300
Sparse Core Ops, SparseCore 0:
  10.7 93.9 all-gather.1
  204.2 17.1 reduce-scatter.1
where the time goes:
time: 231 us; the launch traced here: 230 us
  waiting for transfers between devices  109 us (47%)
  matrix products  31.7 us (14%)
  starting transfers between devices  27.7 us (12%)
  other arithmetic  23.6 us (10%)
  between operations  14.9 us (6%)
  local copies, waits for them, and re-layouts  13.8 us (6%)
  blocking collectives  10.2 us (4%)
    all_gather x1, waiting for transfers between devices, on_device(): members = lax.all_gather(points, 'cent', axis=0, tiled=True)  92 us
    all_to_all x2, starting transfers between devices, group_log_total(): parts = lax.all_to_all(packed, 'cent', 0, 0, tiled=True)  18.1 us
    dot_general x2, matrix products, on_device(): lax.dot_general(weights, half, (((0,), (0,)), ((), ())), preferred_elemen...  17.5 us
    dot_general x2, matrix products, score_block(): lax.dot_general(members, cent_block, (((1,), (1,)), ((), ())), preferred_...  14.2 us
    all_to_all x2, starting transfers between devices, group_log_total(): lax.all_to_all(spread, 'cent', 0, 0, tiled=True)  9.36 us
    reduce_sum x2, other arithmetic, on_device(): local_sum = jnp.sum(jnp.exp(scores - local_max[:, None]), axis=1)  9.06 us
    slice x1, local copies, waits for them, and re-layouts, on_device(): half = split[:, index_h].reshape(cent_count * half_points, feature_width)  8.65 us
    all_to_all x2, waiting for transfers between devices, group_log_total(): lax.all_to_all(spread, 'cent', 0, 0, tiled=True)  7.39 us
  transfers between devices with their start and end apart: 6, of which 4 were waited for; matrix products, arithmetic and copies ran while one was open for 15% of the time, Pallas kernels for 0%

commit v1 on v0

--- a/solution.py
+++ b/solution.py
@@ -37,7 +37,9 @@
     cent_count = lax.axis_size("cent")
     score_scale = 7.0 / math.sqrt(feature_width)
     copies = centroids.astype(jnp.bfloat16)
-    members = lax.all_gather(points, "cent", axis=0, tiled=True)
+    members = jnp.concatenate(
+        lax.all_to_all(jnp.stack([points] * lax.axis_size("cent")), "cent", 0, 0), axis=0
+    )
     gathered = lax.all_gather(copies, "dp", axis=0, tiled=True)
     half_points = own_points // HALVES
     split = members.reshape(cent_count, HALVES, half_points, feature_width)

time: 231 us -> 357 us (1.55)
  waiting for transfers between devices: 109 us -> 215 us
  starting transfers between devices: 27.7 us -> 40.7 us
  local copies, waits for them, and re-layouts: 13.8 us -> 20.7 us
    all_to_all x0 -> x1, waiting for transfers between devices: none -> 200 us  [on_device(): lax.all_to_all(jnp.stack([points] * lax.axis_size('cent')), 'cent', 0, 0)]
    all_gather x1 -> x0, waiting for transfers between devices: 92 us -> none  [on_device(): members = lax.all_gather(points, 'cent', axis=0, tiled=True)]
    all_to_all x0 -> x1, starting transfers between devices: none -> 12.3 us  [on_device(): lax.all_to_all(jnp.stack([points] * lax.axis_size('cent')), 'cent', 0, 0)]
    another operation x0 -> x1, local copies, waits for them, and re-layouts: none -> 6.92 us  [on_device(): jnp.stack([points] * lax.axis_size('cent'))]
  transfers between devices with their start and end apart: 6 -> 6, of which waited for: 4 -> 4; matrix products, arithmetic and copies ran while one was open for 15% -> 10% of each run, Pallas kernels for 0% -> 0%
where the time goes in v1:
time: 357 us; the launch traced here: 356 us
  waiting for transfers between devices  215 us (60%)
  starting transfers between devices  40.7 us (11%)
  matrix products  31.7 us (9%)
  other arithmetic  22.4 us (6%)
  local copies, waits for them, and re-layouts  20.7 us (6%)
  between operations  14.9 us (4%)
  blocking collectives  10.7 us (3%)
    all_to_all x1, waiting for transfers between devices, on_device(): lax.all_to_all(jnp.stack([points] * lax.axis_size('cent')), 'cent', 0, 0)  200 us
    all_to_all x2, starting transfers between devices, group_log_total(): parts = lax.all_to_all(packed, 'cent', 0, 0, tiled=True)  18.8 us
    dot_general x2, matrix products, on_device(): lax.dot_general(weights, half, (((0,), (0,)), ((), ())), preferred_elemen...  17.5 us
    dot_general x2, matrix products, score_block(): lax.dot_general(members, cent_block, (((1,), (1,)), ((), ())), preferred_...  14.2 us
    all_to_all x1, starting transfers between devices, on_device(): lax.all_to_all(jnp.stack([points] * lax.axis_size('cent')), 'cent', 0, 0)  12.3 us
    all_to_all x2, starting transfers between devices, group_log_total(): lax.all_to_all(spread, 'cent', 0, 0, tiled=True)  9.54 us
    reduce_sum x2, other arithmetic, on_device(): local_sum = jnp.sum(jnp.exp(scores - local_max[:, None]), axis=1)  9.06 us
    slice x1, local copies, waits for them, and re-layouts, on_device(): half = split[:, index_h].reshape(cent_count * half_points, feature_width)  8.65 us
  transfers between devices with their start and end apart: 6, of which 4 were waited for; matrix products, arithmetic and copies ran while one was open for 10% of the time, Pallas kernels for 0%

profile of v1, /device:TPU:1, one launch (start us, length us, event | category | flops | bytes accessed | tf_op | source)
XLA Modules:
  0.0 356.2 jit_solution(14049078837834875513)
XLA Ops:
  7.2 6.9 %stack.6 = bf16[64,128,768]{2,1,0:T(8,128)(2,1)} broadcast(bf16[128,768]{1,0:T(8,128)(2,1)} %param.2), dimensions={1,2} | broadcast | bytes 12779520 | tf_op jit(solution)/shard_map/stack | solution.py:41
  14.1 12.3 %all-to-all-start = ((bf16[64,128,768]{2,1,0:T(8,128)(2,1)}), bf16[64,128,768]{2,1,0:T(8,128)(2,1)}, u32[]{:S(2)}, u32[]{:S(2)}) async-start(bf16[64,128,768]{2,1,0:T(8,128)(2,1)} %stack.6), calls=%async_computation | async-start | bytes 25165824 | tf_op jit(solution)/shard_map/all_to_all | solution.py:41
  26.5 3.0 all_gather.3
  29.6 199.5 %all-to-all-done = bf16[64,128,768]{2,1,0:T(8,128)(2,1)} async-done(((bf16[64,128,768]{2,1,0:T(8,128)(2,1)}), bf16[64,128,768]{2,1,0:T(8,128)(2,1)}, u32[]{:S(2)}, u32[]{:S(2)}) %all-to-all-start) | async-done | bytes 12582944 | tf_op jit(solution)/shard_map/all_to_all | solution.py:41
  229.2 8.6 %fusion.1 = (bf16[64,1,64,768]{3,2,1,0:T(8,128)(2,1)}, bf16[64,1,64,768]{3,2,1,0:T(8,128)(2,1)S(1)}) fusion(bf16[64,2,64,768]{3,2,1,0:T(8,128)(2,1)} %bitcast), kind=kLoop, calls=%fused_computation.20 | loop fusion | bytes 25165824 | tf_op jit(solution)/shard_map/slice | solution.py:50
  237.8 5.8 %fusion.4 = (f32[4096]{0:T(1024)S(1)}, f32[4096,512]{0,1:T(8,128)}) fusion(f32[512]{0:T(512)S(1)} %multiply_reduce_fusion, bf16[4096,768]{1,0:T(8,128)(2,1)S(1)} %bitcast.20, bf16[512,768]{1,0:T(8,128)(2,1)S(1)} %all_gather.3), kind=kOutput, calls=%fused_computation.23 | convolution fusion | flops 3229609984 | bytes 15484928 | tf_op jit(solution)/shard_map/dot_general | solution.py:12
  243.7 4.5 %exponential_reduce_fusion.1 = f32[4096]{0:T(1024)S(1)} fusion(f32[4096,512]{0,1:T(8,128)} %get-tuple-element.9, f32[4096]{0:T(1024)S(1)} %get-tuple-element.8), kind=kLoop, calls=%fused_computation.6 | loop fusion | flops 4190208 | bytes 8421376 | tf_op jit(solution)/shard_map/reduce_sum | solution.py:53
  248.4 0.7 reshape.58
  249.1 9.0 %all-to-all-start.1 = ((f32[64,1,128]{2,1,0:T(1,128)}), f32[64,1,128]{2,1,0:T(1,128)S(1)}, u32[]{:S(2)}, u32[]{:S(2)}) async-start(f32[64,1,128]{2,1,0:T(1,128)} %reshape.58), calls=%async_computation.1 | async-start | bytes 65536 | tf_op jit(solution)/shard_map/all_to_all | solution.py:24
  258.1 8.5 %fusion.5 = (f32[4096]{0:T(1024)S(1)}, f32[4096,512]{0,1:T(8,128)}) fusion(f32[512]{0:T(512)S(1)} %multiply_reduce_fusion, bf16[4096,768]{1,0:T(8,128)(2,1)} %bitcast.18, bf16[512,768]{1,0:T(8,128)(2,1)S(1)} %all_gather.3), kind=kOutput, calls=%fused_computation.24 | convolution fusion | flops 3229609984 | bytes 15484928 | tf_op jit(solution)/shard_map/dot_general | solution.py:12
  266.7 4.5 %exponential_reduce_fusion = f32[4096]{0:T(1024)S(1)} fusion(f32[4096,512]{0,1:T(8,128)} %get-tuple-element.11, f32[4096]{0:T(1024)S(1)} %get-tuple-element.10), kind=kLoop, calls=%fused_computation.3 | loop fusion | flops 4190208 | bytes 8421376 | tf_op jit(solution)/shard_map/reduce_sum | solution.py:53
  271.4 0.7 reshape.60
  272.1 9.8 %all-to-all-start.3 = ((f32[64,1,128]{2,1,0:T(1,128)}), f32[64,1,128]{2,1,0:T(1,128)S(1)}, u32[]{:S(2)}, u32[]{:S(2)}) async-start(f32[64,1,128]{2,1,0:T(1,128)} %reshape.60), calls=%async_computation.3 | async-start | bytes 65536 | tf_op jit(solution)/shard_map/all_to_all | solution.py:24
  281.9 0.5 broadcast.37
  282.4 0.7 reduce.10
  283.4 7.0 %all-to-all-done.3 = f32[64,1,128]{2,1,0:T(1,128)S(1)} async-done(((f32[64,1,128]{2,1,0:T(1,128)}), f32[64,1,128]{2,1,0:T(1,128)S(1)}, u32[]{:S(2)}, u32[]{:S(2)}) %all-to-all-start.3) | async-done | bytes 32800 | tf_op jit(solution)/shard_map/all_to_all | solution.py:24
  290.3 0.6 broadcast_in_dim.4
  291.0 4.7 %all-to-all-start.2 = ((f32[64,1,64]{2,1,0:T(1,128)}), f32[64,1,64]{2,1,0:T(1,128)S(1)}, u32[]{:S(2)}, u32[]{:S(2)}) async-start(f32[64,1,64]{2,1,0:T(1,128)} %broadcast_in_dim.4), calls=%async_computation.2 | async-start | bytes 65536 | tf_op jit(solution)/shard_map/all_to_all | solution.py:30
  295.7 0.7 reduce.11
  296.6 7.4 %all-to-all-done.2 = f32[64,1,64]{2,1,0:T(1,128)S(1)} async-done(((f32[64,1,64]{2,1,0:T(1,128)}), f32[64,1,64]{2,1,0:T(1,128)S(1)}, u32[]{:S(2)}, u32[]{:S(2)}) %all-to-all-start.2) | async-done | bytes 16416 | tf_op jit(solution)/shard_map/all_to_all | solution.py:30
  304.0 0.6 broadcast_in_dim.5
  304.7 4.9 %all-to-all-start.4 = ((f32[64,1,64]{2,1,0:T(1,128)}), f32[64,1,64]{2,1,0:T(1,128)S(1)}, u32[]{:S(2)}, u32[]{:S(2)}) async-start(f32[64,1,64]{2,1,0:T(1,128)} %broadcast_in_dim.5), calls=%async_computation.4 | async-start | bytes 65536 | tf_op jit(solution)/shard_map/all_to_all | solution.py:30
  310.1 0.7 reduce.8
  310.9 7.7 %fusion = f32[512,768]{1,0:T(8,128)S(1)} fusion(bf16[4096,768]{1,0:T(8,128)(2,1)} %bitcast.21, f32[4096,512]{0,1:T(8,128)} %get-tuple-element.9, f32[4096]{0:T(1024)S(1)} %sub.72), kind=kOutput, calls=%fused_computation.10 | convolution fusion | flops 3225419776 | bytes 16269312 | tf_op jit(solution)/shard_map/dot_general | solution.py:57
  318.6 0.7 reduce.9
  319.4 9.8 %convolution_add_fusion = f32[512,768]{1,0:T(8,128)} fusion(f32[512,768]{1,0:T(8,128)S(1)} %fusion, bf16[4096,768]{1,0:T(8,128)(2,1)} %bitcast.19, f32[4096,512]{0,1:T(8,128)} %get-tuple-element.11, f32[4096]{0:T(1024)S(1)} %sub.80), kind=kOutput, calls=%fused_computation.9 | convolution fusion | flops 3225812992 | bytes 17842176 | tf_op jit(solution)/shard_map/dot_general | solution.py:57
  329.2 0.6 dynamic-slice
  330.5 0.6 pad_maximum_fusion.2
  331.1 7.1 %convert_reduce_fusion = (f32[512]{0:T(512)S(1)}, f32[512]{0:T(512)S(1)}) fusion(f32[4096,512]{0,1:T(8,128)} %get-tuple-element.11, f32[4096]{0:T(1024)S(1)} %sub.80, f32[4096,512]{0,1:T(8,128)} %get-tuple-element.9, f32[4096]{0:T(1024)S(1)} %sub.72), kind=kLoop, calls=%fused_computation | loop fusion | flops 16776192 | bytes 16814080 | tf_op jit(solution)/shard_map/reduce_sum | solution.py:60
  338.1 7.7 %all-reduce = f32[512]{0:T(512)S(1)} all-reduce(f32[512]{0:T(512)S(1)} %add.38), channel_id=3, replica_groups=mesh['dp'=2,'cent'=64] {'dp'}, use_global_device_ids=true, to_apply=%region_12.0.clone | all-reduce | flops 512 | bytes 4096
  345.9 1.3 reduce-scatter.2.cloned.1.call-done
  347.2 2.1 add_divide_fusion
  (33 shorter events, 2.0 us)
Async XLA Ops:
  14.1 12.3 %copy-start.1 = (f32[256,768]{1,0:T(8,128)S(1)}, f32[256,768]{1,0:T(8,128)}, u32[]{:S(2)}) copy-start(f32[256,768]{1,0:T(8,128)} %param.3) | copy-start | bytes 2359300
  14.1 215.1 %all-to-all-start = ((bf16[64,128,768]{2,1,0:T(8,128)(2,1)}), bf16[64,128,768]{2,1,0:T(8,128)(2,1)}, u32[]{:S(2)}, u32[]{:S(2)}) async-start(bf16[64,128,768]{2,1,0:T(8,128)(2,1)} %stack.6), calls=%async_computation | async-start | bytes 25165824 | tf_op jit(solution)/shard_map/all_to_all | solution.py:41
  237.8 5.8 %copy-start = (bf16[64,1,64,768]{3,2,1,0:T(8,128)(2,1)}, bf16[64,1,64,768]{3,2,1,0:T(8,128)(2,1)S(1)}, u32[]{:S(2)}) copy-start(bf16[64,1,64,768]{3,2,1,0:T(8,128)(2,1)S(1)} %get-tuple-element.3) | copy-start | bytes 18874372
  249.1 23.0 %all-to-all-start.1 = ((f32[64,1,128]{2,1,0:T(1,128)}), f32[64,1,128]{2,1,0:T(1,128)S(1)}, u32[]{:S(2)}, u32[]{:S(2)}) async-start(f32[64,1,128]{2,1,0:T(1,128)} %reshape.58), calls=%async_computation.1 | async-start | bytes 65536 | tf_op jit(solution)/shard_map/all_to_all | solution.py:24
  272.1 18.2 %all-to-all-start.3 = ((f32[64,1,128]{2,1,0:T(1,128)}), f32[64,1,128]{2,1,0:T(1,128)S(1)}, u32[]{:S(2)}, u32[]{:S(2)}) async-start(f32[64,1,128]{2,1,0:T(1,128)} %reshape.60), calls=%async_computation.3 | async-start | bytes 65536 | tf_op jit(solution)/shard_map/all_to_all | solution.py:24
  291.0 13.0 %all-to-all-start.2 = ((f32[64,1,64]{2,1,0:T(1,128)}), f32[64,1,64]{2,1,0:T(1,128)S(1)}, u32[]{:S(2)}, u32[]{:S(2)}) async-start(f32[64,1,64]{2,1,0:T(1,128)} %broadcast_in_dim.4), calls=%async_computation.2 | async-start | bytes 65536 | tf_op jit(solution)/shard_map/all_to_all | solution.py:30
  304.7 14.0 %all-to-all-start.4 = ((f32[64,1,64]{2,1,0:T(1,128)}), f32[64,1,64]{2,1,0:T(1,128)S(1)}, u32[]{:S(2)}, u32[]{:S(2)}) async-start(f32[64,1,64]{2,1,0:T(1,128)} %broadcast_in_dim.5), calls=%async_computation.4 | async-start | bytes 65536 | tf_op jit(solution)/shard_map/all_to_all | solution.py:30
  309.5 37.7 %reduce-scatter.2.cloned.1.call-start = ((), (), s32[]{:S(2)}) async-start(), calls=%async_computation.6 | async-start | bytes 2359296 | tf_op jit(solution)/shard_map/reduce_scatter | solution.py:63
  319.4 9.8 %copy-start.2 = (u32[128]{0:T(128)S(1)}, u32[128]{0:T(128)}, u32[]{:S(2)}) copy-start(u32[128]{0:T(128)} %constant.12) | copy-start | bytes 1540
Sparse Core Ops, SparseCore 0:
  329.3 17.8 reduce-scatter.1
